TPU v7x, 32 devices: a whole 2x2x4 slice. The times are simulated.
32 devices in a mesh: scan: 16 (over z, y, core), row: 2 (over x).
Axes of the slice: x: 2, y: 2, z: 4, core: 2. Of those that a mesh axis runs over, the one named last changes fastest.
Arguments:
- estimate: float32 [128, 64, 512], P('scan', 'row'), may hold values from -6 to 6
- raw: float32 [128, 64, 512], P('scan', 'row'), may hold values from -6 to 6
- offsets: int32 [128], replicated, may hold values from 0 to 16, as said below
- depth_psf: float32 [64], replicated, may hold values from 0.03 to 0.2
- lateral_psf: float32 [17], replicated, may hold values from 0.05 to 0.4
- step_size: float32 [1], replicated, may hold values from 0.3 to 0.8
- threshold: float32 [1], replicated, may hold values from 0.3 to 1.5
Outputs:
- new_estimate: float32 [128, 64, 512], P('scan', 'row')
- misfit: float32 [128, 64, 512], P('scan', 'row')
Inputs may be any that keep to these rules, and one draw needn't show every extreme that they name: offsets[p] is how many planes beyond p the sheet of scan plane p begins; both 0 and 16 occur.
All inputs are finite; a program needn't handle non-finite values.
Results may differ from a plain program's by a relative error of at most 0.0003.
Values sent between devices are 32-bit elements; how exact they have to be, the bound alone decides.
No kernel may reach another device: no remote copies, remote signals or barrier semaphores. Data moves between devices by JAX's collectives and lax.ppermute only.
A program may use at most 64 MiB of HBM per device.

v0:
```python
import jax
import jax.numpy as jnp
from jax import lax
from jax.sharding import PartitionSpec as P

highest_mode = lax.Precision.HIGHEST


def with_halo(cells, axis, width):
    count = lax.axis_size(axis)
    head = lax.slice_in_dim(cells, 0, width, axis=1)
    tail = lax.slice_in_dim(cells, cells.shape[1] - width, cells.shape[1], axis=1)
    zeros = jnp.zeros_like(head)
    if count == 2:
        first = lax.axis_index(axis) == 0
        arrived = lax.ppermute(jnp.where(first, tail, head), axis, [(0, 1), (1, 0)])
        above = jnp.where(first, zeros, arrived)
        below = jnp.where(first, arrived, zeros)
    else:
        ends = count - 1
        above = lax.ppermute(tail, axis, [(i, (i + 1) % count) for i in range(ends)])
        below = lax.ppermute(head, axis, [((i + 1) % count, i) for i in range(ends)])
    return jnp.concatenate([above, cells, below], axis=1)


def band_matrix(kernel_taps, row_count, shift):
    tap_count = kernel_taps.shape[0]
    out_rows = jnp.arange(row_count, dtype=jnp.int32)[:, None]
    in_rows = jnp.arange(row_count + tap_count - 1, dtype=jnp.int32)[None, :]
    lag = shift + in_rows - out_rows
    taps = jnp.arange(tap_count, dtype=jnp.int32)
    return jnp.sum(jnp.where(lag[:, :, None] == taps, kernel_taps, 0.0), axis=-1)


def lateral_apply(band, padded):
    return jnp.einsum("rk,pkc->prc", band, padded, precision=highest_mode)


def sheet_matrix(own_offsets, depth_psf, column_count):
    plane_rows = jnp.arange(own_offsets.shape[0], dtype=jnp.int32)[:, None]
    plane_columns = jnp.arange(column_count, dtype=jnp.int32)[None, :]
    lag_planes = plane_columns - plane_rows - own_offsets[:, None]
    depth_count = depth_psf.shape[0]
    inside = (lag_planes >= 0) & (lag_planes < depth_count)
    taps = jnp.arange(depth_count, dtype=jnp.int32)
    picked = jnp.where(lag_planes[:, :, None] == taps, depth_psf, 0.0)
    return jnp.where(inside, jnp.sum(picked, axis=-1), 0.0)


def transpose_apply(sheet_psf, values):
    return lax.dot_general(sheet_psf, values, (((0,), (0,)), ((), ())), precision=highest_mode)


def body(estimate, raw, offsets, depth_psf, lateral_psf, step_size, threshold):
    plane_count, row_count, width_count = estimate.shape
    flat_count = row_count * width_count
    halo_rows = lateral_psf.shape[0] // 2
    sheet_psf = sheet_matrix(offsets, depth_psf, offsets.shape[0])
    blur_band = band_matrix(lateral_psf, row_count, 0)
    back_band = band_matrix(lateral_psf[::-1], row_count, 0)
    padded = with_halo(estimate, "row", halo_rows)
    blurred = lateral_apply(blur_band, padded).reshape(plane_count, flat_count)
    both_flat = jnp.stack([blurred, raw.reshape(plane_count, flat_count)])
    both_in = lax.all_to_all(both_flat, "scan", split_axis=2, concat_axis=1, tiled=True)
    pencil = both_in[0]
    raw_pencil = both_in[1]
    predicted_pencil = jnp.dot(sheet_psf, pencil, precision=highest_mode)
    misfit_pencil = predicted_pencil - raw_pencil
    back_pencil = transpose_apply(sheet_psf, misfit_pencil)
    both_out = lax.all_to_all(
        jnp.stack([misfit_pencil, back_pencil]), "scan", split_axis=1, concat_axis=2, tiled=True
    )
    misfit = both_out[0]
    back_volume = both_out[1].reshape(plane_count, row_count, width_count)
    padded_back = with_halo(back_volume, "row", halo_rows)
    gradient = lateral_apply(back_band, padded_back)
    stepped = estimate - step_size[0] * gradient
    shrink_level = step_size[0] * threshold[0]
    new_estimate = jnp.sign(stepped) * jnp.maximum(jnp.abs(stepped) - shrink_level, 0.0)
    return (new_estimate, misfit.reshape(plane_count, row_count, width_count))


def solution(mesh):
    placed = (P("scan", "row", None), P("scan", "row", None), P(), P(), P(), P(), P())
    return jax.shard_map(
        body,
        mesh=mesh,
        in_specs=placed,
        out_specs=(P("scan", "row", None), P("scan", "row", None)),
        check_vma=False,
    )
```

profile of v0, /device:TPU:0, one launch (start us, length us, event | category | flops | bytes accessed | tf_op | source)
XLA Modules:
  0.0 181.3 jit_solution(13650661179167656259)
XLA Ops:
  0.6 1.0 slice_select_fusion.1
  1.6 3.0 %collective-permute-start = (f32[8,8,512]{2,1,0:T(8,128)S(1)}, f32[8,8,512]{2,1,0:T(8,128)S(1)}, u32[]{:S(2)}, u32[]{:S(2)}) collective-permute-start(f32[8,8,512]{2,1,0:T(8,128)S(1)} %slice_select_fusion.1), channel_id=1, source_target_pairs={{0,1},{1,0},{2,3},{3,2},{4,5},{5,4},{6,7},{7,6},{8,9},{9,8},{10,11... | collective-permute-start | bytes 393224 | tf_op jit(solution)/shard_map/ppermute | solution.py:16
  4.6 0.7 rev.3
  5.4 1.1 stack_reshape.7
  6.5 0.8 select_reduce_fusion.1
  7.3 0.8 collective-permute-done
  8.2 1.7 convolution_bitcast_fusion.1
  9.9 0.1 stack_reshape.6
  10.0 0.1 pad_maximum_fusion
  10.0 14.6 %copy.19 = f32[2,8,16384]{1,0,2:T(2,128)} copy(f32[2,8,16384]{2,1,0:T(8,128)S(1)} %pad_maximum_fusion) | data formatting | bytes 2097152 | tf_op jit(solution)/shard_map/stack | solution.py:63
  24.6 29.0 %reshape.53 = f32[16,1,16384]{2,1,0:T(1,128)} reshape(f32[16384,2,8]{2,1,0:T(2,128)} %bitcast.42) | data formatting | bytes 2097152
  53.6 6.2 %all-to-all-start = ((f32[16,1,16384]{2,1,0:T(1,128)}), f32[16,1,16384]{2,1,0:T(1,128)S(1)}, u32[]{:S(2)}, u32[]{:S(2)}) async-start(f32[16,1,16384]{2,1,0:T(1,128)} %reshape.53), calls=%async_computation | async-start | bytes 2097152 | tf_op jit(solution)/shard_map/all_to_all | solution.py:64
  59.8 0.1 subtract_subtract_fusion
  59.9 1.4 select_reduce_fusion
  61.3 21.5 %all-to-all-done = f32[16,1,16384]{2,1,0:T(1,128)S(1)} async-done(((f32[16,1,16384]{2,1,0:T(1,128)}), f32[16,1,16384]{2,1,0:T(1,128)S(1)}, u32[]{:S(2)}, u32[]{:S(2)}) %all-to-all-start) | async-done | bytes 1048608 | tf_op jit(solution)/shard_map/all_to_all | solution.py:64
  82.8 0.5 broadcast.33
  83.3 3.1 %reduce = f32[16,16384]{1,0:T(8,128)S(1)} reduce(f32[16,1,16384]{2,1,0:T(1,128)S(1)} %all-to-all-done, f32[]{:T(128)} %broadcast.33), dimensions={1}, to_apply=%all_to_all.22.reduce_sub_computation | reduce | bytes 2097156 | tf_op jit(solution)/shard_map/all_to_all | solution.py:64
  86.4 31.9 %reshape.54 = f32[16384,2,8]{2,1,0:T(2,128)} reshape(f32[16,16384]{1,0:T(8,128)S(1)} %reduce) | data formatting | bytes 2097152
  118.4 20.3 %copy.20 = f32[2,8,16,1024]{3,1,2,0:T(8,128)S(1)} copy(f32[2,8,16,1024]{1,0,3,2:T(2,128)} %bitcast.43) | data formatting | bytes 2097152 | tf_op jit(solution)/shard_map/all_to_all | solution.py:64
  138.7 0.6 convolution_subtract_fusion
  139.3 0.7 convolution_bitcast_fusion
  140.0 0.1 pad_maximum_fusion.1
  140.1 0.8 copy.21
  140.9 0.0 copy-start
  141.0 31.6 %all_to_all.30 = f32[2,128,1024]{2,0,1:T(2,128)S(1)} all-to-all(f32[2,128,1024]{2,0,1:T(2,128)S(1)} %copy.21), channel_id=1, replica_groups=mesh['scan'=16,'row'=2] {'scan'}, dimensions={1} | all-to-all | bytes 2097152 | tf_op jit(solution)/shard_map/all_to_all | solution.py:70
  172.6 0.6 copy.24
  173.2 0.1 fusion.24
  173.3 0.1 reshape_squeeze.6
  173.4 1.6 collective-permute-start.1
  176.3 0.9 reshape_squeeze.7
  177.1 2.5 %collective-permute-done.1 = f32[8,8,512]{2,1,0:T(8,128)S(1)} collective-permute-done((f32[8,8,512]{2,1,0:T(8,128)S(1)}, f32[8,8,512]{2,1,0:T(8,128)S(1)}, u32[]{:S(2)}, u32[]{:S(2)}) %collective-permute-start.1) | collective-permute-done | bytes 131104 | tf_op jit(solution)/shard_map/ppermute | solution.py:16
  179.7 1.6 maximum_multiply_fusion
  (9 shorter events, 0.1 us)
Async XLA Ops:
  1.6 6.5 %collective-permute-start = (f32[8,8,512]{2,1,0:T(8,128)S(1)}, f32[8,8,512]{2,1,0:T(8,128)S(1)}, u32[]{:S(2)}, u32[]{:S(2)}) collective-permute-start(f32[8,8,512]{2,1,0:T(8,128)S(1)} %slice_select_fusion.1), channel_id=1, source_target_pairs={{0,1},{1,0},{2,3},{3,2},{4,5},{5,4},{6,7},{7,6},{8,9},{9,8},{10,11... | collective-permute-start | bytes 393224 | tf_op jit(solution)/shard_map/ppermute | solution.py:16
  24.6 35.2 %copy-start.1 = (s32[128]{0:T(128)S(1)}, s32[128]{0:T(128)}, u32[]{:S(2)}) copy-start(s32[128]{0:T(128)} %param.9) | copy-start | bytes 1540
  24.6 35.3 %copy-start.2 = (f32[64]{0:T(128)S(1)}, f32[64]{0:T(128)}, u32[]{:S(2)}) copy-start(f32[64]{0:T(128)} %param.10) | copy-start | bytes 772
  53.6 29.1 %all-to-all-start = ((f32[16,1,16384]{2,1,0:T(1,128)}), f32[16,1,16384]{2,1,0:T(1,128)S(1)}, u32[]{:S(2)}, u32[]{:S(2)}) async-start(f32[16,1,16384]{2,1,0:T(1,128)} %reshape.53), calls=%async_computation | async-start | bytes 2097152 | tf_op jit(solution)/shard_map/all_to_all | solution.py:64
  140.9 38.7 %copy-start = (f32[8,32,512]{2,1,0:T(8,128)S(1)}, f32[8,32,512]{2,1,0:T(8,128)}, u32[]{:S(2)}) copy-start(f32[8,32,512]{2,1,0:T(8,128)} %param.7) | copy-start | bytes 1572868
  173.4 6.2 %collective-permute-start.1 = (f32[8,8,512]{2,1,0:T(8,128)S(1)}, f32[8,8,512]{2,1,0:T(8,128)S(1)}, u32[]{:S(2)}, u32[]{:S(2)}) collective-permute-start(f32[8,8,512]{2,1,0:T(8,128)S(1)} %slice_select_fusion), channel_id=1, source_target_pairs={{0,1},{1,0},{2,3},{3,2},{4,5},{5,4},{6,7},{7,6},{8,9},{9,8},{10,11... | collective-permute-start | bytes 393224 | tf_op jit(solution)/shard_map/ppermute | solution.py:16
where the time goes:
time: 182 us; the launch traced here: 181 us
  local copies, waits for them, and re-layouts  101 us (55%)
  blocking collectives  31.6 us (17%)
  waiting for transfers between devices  24.8 us (14%)
  starting transfers between devices  10.8 us (6%)
  other arithmetic  6.57 us (4%)
  matrix products  4.67 us (3%)
  between operations  2.12 us (1%)
    unnamed x8, local copies, waits for them, and re-layouts  60.9 us
    all_to_all x1, blocking collectives, body(): lax.all_to_all(jnp.stack([misfit_pencil, back_pencil]), 'scan', split_axi...  31.6 us
    all_to_all x1, waiting for transfers between devices, body(): lax.all_to_all(both_flat, 'scan', split_axis=2, concat_axis=1, tiled=True)  21.5 us
    all_to_all x2, local copies, waits for them, and re-layouts, body(): lax.all_to_all(both_flat, 'scan', split_axis=2, concat_axis=1, tiled=True)  20.8 us
    another operation x3, local copies, waits for them, and re-layouts, body(): both_flat = jnp.stack([blurred, raw.reshape(plane_count, flat_count)])  15.8 us
    all_to_all x1, starting transfers between devices, body(): lax.all_to_all(both_flat, 'scan', split_axis=2, concat_axis=1, tiled=True)  6.2 us
    ppermute x2, starting transfers between devices, with_halo(): arrived = lax.ppermute(jnp.where(first, tail, head), axis, [(0, 1), (1, 0)])  4.56 us
  transfers between devices with their start and end apart: 3, of which 3 were waited for; matrix products, arithmetic and copies ran while one was open for 3% of the time, Pallas kernels for 0%

commit v1 on v0

--- a/solution.py
+++ b/solution.py
@@ -4,6 +4,29 @@
 from jax.sharding import PartitionSpec as P
 
 highest_mode = lax.Precision.HIGHEST
+
+
+def in_blocks(shard, dim, size):
+    dims = shard.shape
+    tiles = shard.reshape(*dims[:dim], size, dims[dim] // size, *dims[dim + 1 :])
+    return jnp.moveaxis(tiles, dim, 0)
+
+
+def laid_out(blocks, dim):
+    dims = list(blocks.shape[1:])
+    dims[dim] *= blocks.shape[0]
+    return jnp.moveaxis(blocks, 0, dim).reshape(dims)
+
+
+def swapped_with_each(shard, axis, split_dim, concat_dim):
+    size, here = (lax.axis_size(axis), lax.axis_index(axis))
+    pieces = in_blocks(shard, split_dim, size)
+    done = [pieces[here]]
+    for step in range(1, size):
+        sent = pieces[here ^ step]
+        done.append(lax.ppermute(sent, axis, [(i, i ^ step) for i in range(size)]))
+    pieces = jnp.stack(done)[here ^ jnp.arange(size)]
+    return laid_out(pieces, concat_dim)
 
 
 def with_halo(cells, axis, width):
@@ -61,7 +84,7 @@
     padded = with_halo(estimate, "row", halo_rows)
     blurred = lateral_apply(blur_band, padded).reshape(plane_count, flat_count)
     both_flat = jnp.stack([blurred, raw.reshape(plane_count, flat_count)])
-    both_in = lax.all_to_all(both_flat, "scan", split_axis=2, concat_axis=1, tiled=True)
+    both_in = swapped_with_each(both_flat, "scan", 2, 1)
     pencil = both_in[0]
     raw_pencil = both_in[1]
     predicted_pencil = jnp.dot(sheet_psf, pencil, precision=highest_mode)

time: 182 us -> 85.7 us (0.47)
  local copies, waits for them, and re-layouts: 101 us -> 5.85 us
  starting transfers between devices: 10.8 us -> 29.2 us
  waiting for transfers between devices: 24.8 us -> 9.76 us
  other arithmetic: 6.57 us -> 4.07 us
    unnamed x8 -> x39, local copies, waits for them, and re-layouts: 60.9 us -> 0.4 us
    ppermute x0 -> x15, starting transfers between devices: none -> 24.8 us  [swapped_with_each(): done.append(lax.ppermute(sent, axis, [(i, i ^ step) for i in range(size)]))]
    all_to_all x1 -> x0, waiting for transfers between devices: 21.5 us -> none  [body(): lax.all_to_all(both_flat, 'scan', split_axis=2, concat_axis=1, tiled=True)]
    all_to_all x2 -> x0, local copies, waits for them, and re-layouts: 20.8 us -> none  [body(): lax.all_to_all(both_flat, 'scan', split_axis=2, concat_axis=1, tiled=True)]
    another operation x3, local copies, waits for them, and re-layouts: 15.8 us -> 0.38 us  [body(): both_flat = jnp.stack([blurred, raw.reshape(plane_count, flat_count)])]
    ppermute x0 -> x15, waiting for transfers between devices: none -> 7 us  [swapped_with_each(): done.append(lax.ppermute(sent, axis, [(i, i ^ step) for i in range(size)]))]
    all_to_all x1 -> x0, starting transfers between devices: 6.2 us -> none  [body(): lax.all_to_all(both_flat, 'scan', split_axis=2, concat_axis=1, tiled=True)]
    all_to_all x1 -> x0, other arithmetic: 3.15 us -> none  [body(): lax.all_to_all(both_flat, 'scan', split_axis=2, concat_axis=1, tiled=True)]
  transfers between devices with their start and end apart: 3 -> 17, of which waited for: 3 -> 6; matrix products, arithmetic and copies ran while one was open for 3% -> 6% of each run, Pallas kernels for 0% -> 0%
where the time goes in v1:
time: 85.7 us; the launch traced here: 85.5 us
  blocking collectives  30.6 us (36%)
  starting transfers between devices  29.2 us (34%)
  waiting for transfers between devices  9.76 us (11%)
  local copies, waits for them, and re-layouts  5.85 us (7%)
  other arithmetic  4.07 us (5%)
  matrix products  3.62 us (4%)
  between operations  2.48 us (3%)
    all_to_all x1, blocking collectives, body(): lax.all_to_all(jnp.stack([misfit_pencil, back_pencil]), 'scan', split_axi...  30.6 us
    ppermute x15, starting transfers between devices, swapped_with_each(): done.append(lax.ppermute(sent, axis, [(i, i ^ step) for i in range(size)]))  24.8 us
    ppermute x15, waiting for transfers between devices, swapped_with_each(): done.append(lax.ppermute(sent, axis, [(i, i ^ step) for i in range(size)]))  7 us
    ppermute x2, starting transfers between devices, with_halo(): arrived = lax.ppermute(jnp.where(first, tail, head), axis, [(0, 1), (1, 0)])  4.31 us
    ppermute x2, waiting for transfers between devices, with_halo(): arrived = lax.ppermute(jnp.where(first, tail, head), axis, [(0, 1), (1, 0)])  2.76 us
    dot_general x2, matrix products, lateral_apply(): return jnp.einsum('rk,pkc->prc', band, padded, precision=highest_mode)  2.29 us
    reduce_sum x1, other arithmetic, sheet_matrix(): return jnp.where(inside, jnp.sum(picked, axis=-1), 0.0)  1.99 us
  transfers between devices with their start and end apart: 17, of which 6 were waited for; matrix products, arithmetic and copies ran while one was open for 6% of the time, Pallas kernels for 0%

profile of v1, /device:TPU:0, one launch (start us, length us, event | category | flops | bytes accessed | tf_op | source)
XLA Modules:
  0.0 85.5 jit_solution(11764757607683127562)
XLA Ops:
  0.7 1.1 %slice_select_fusion.1 = f32[8,8,512]{2,1,0:T(8,128)S(1)} fusion(f32[8,32,512]{2,1,0:T(8,128)} %param.7, pred[]{:T(512)S(6)} %eq.20), kind=kLoop, calls=%fused_computation.28 | loop fusion | flops 32768 | bytes 393217 | tf_op jit(solution)/shard_map/jit(_where)/select_n | solution.py:39
  1.7 3.0 %collective-permute-start = (f32[8,8,512]{2,1,0:T(8,128)S(1)}, f32[8,8,512]{2,1,0:T(8,128)S(1)}, u32[]{:S(2)}, u32[]{:S(2)}) collective-permute-start(f32[8,8,512]{2,1,0:T(8,128)S(1)} %slice_select_fusion.1), channel_id=1, source_target_pairs={{0,1},{1,0},{2,3},{3,2},{4,5},{5,4},{6,7},{7,6},{8,9},{9,8},{10,11... | collective-permute-start | bytes 393224 | tf_op jit(solution)/shard_map/ppermute | solution.py:39
  4.8 0.7 subtract_subtract_fusion
  5.5 2.0 %select_reduce_fusion = f32[128,128]{1,0:T(8,128)S(1)} fusion(f32[64]{0:T(128)} %param.10, s32[128,128]{1,0:T(8,128)S(1)} %subtract_subtract_fusion), kind=kLoop, calls=%fused_computation.1 | loop fusion | flops 3129344 | bytes 131328 | tf_op jit(solution)/shard_map/reduce_sum | solution.py:70
  7.6 0.7 rev.3
  8.8 0.6 convolution_bitcast_fusion.1
  9.7 1.3 %constant_dynamic-slice_fusion = (f32[2,8,1,1024]{3,2,1,0:T(1,128)S(1)}, f32[2,8,1,1024]{3,2,1,0:T(1,128)S(1)}, f32[2,8,1,1024]{3,2,1,0:T(1,128)S(1)}, f32[2,8,1...) fusion(f32[2,8,16,1024]{3,2,1,0:T(8,128)S(1)} %constant_dynamic, ...), kind=kLoop, calls=%fused_computation.73 | loop fusion | bytes 2097216 | tf_op jit(solution)/shard_map/dynamic-slice.15
  11.1 1.6 %collective-permute-start.2 = (f32[2,8,1024]{2,1,0:T(8,128)S(1)}, f32[2,8,1024]{2,1,0:T(8,128)S(1)}, u32[]{:S(2)}, u32[]{:S(2)}) collective-permute-start(f32[2,8,1024]{2,1,0:T(8,128)S(1)} %bitcast.135), channel_id=1, source_target_pairs={{0,4},{2,6},{4,0},{6,2},{8,12},{10,14},{12,8},{14,10},{16,20},{18,... | collective-permute-start | bytes 196616 | tf_op jit(solution)/shard_map/ppermute | solution.py:27
  12.7 0.4 collective-permute-start.3
  13.1 1.6 %collective-permute-start.4 = (f32[2,8,1024]{2,1,0:T(8,128)S(1)}, f32[2,8,1024]{2,1,0:T(8,128)S(1)}, u32[]{:S(2)}, u32[]{:S(2)}) collective-permute-start(f32[2,8,1024]{2,1,0:T(8,128)S(1)} %bitcast.133), channel_id=1, source_target_pairs={{0,8},{2,10},{4,12},{6,14},{8,0},{10,2},{12,4},{14,6},{16,24},{18,... | collective-permute-start | bytes 196616 | tf_op jit(solution)/shard_map/ppermute | solution.py:27
  15.2 2.6 %collective-permute-start.6 = (f32[2,8,1024]{2,1,0:T(8,128)S(1)}, f32[2,8,1024]{2,1,0:T(8,128)S(1)}, u32[]{:S(2)}, u32[]{:S(2)}) collective-permute-start(f32[2,8,1024]{2,1,0:T(8,128)S(1)} %bitcast.131), channel_id=1, source_target_pairs={{0,12},{2,14},{4,8},{6,10},{8,4},{10,6},{12,0},{14,2},{16,28},{18,... | collective-permute-start | bytes 196616 | tf_op jit(solution)/shard_map/ppermute | solution.py:27
  18.1 2.7 %collective-permute-start.8 = (f32[2,8,1024]{2,1,0:T(8,128)S(1)}, f32[2,8,1024]{2,1,0:T(8,128)S(1)}, u32[]{:S(2)}, u32[]{:S(2)}) collective-permute-start(f32[2,8,1024]{2,1,0:T(8,128)S(1)} %bitcast.129), channel_id=1, source_target_pairs={{0,16},{2,18},{4,20},{6,22},{8,24},{10,26},{12,28},{14,30},{16,0},... | collective-permute-start | bytes 196616 | tf_op jit(solution)/shard_map/ppermute | solution.py:27
  20.7 0.4 collective-permute-start.9
  21.2 3.2 %collective-permute-start.10 = (f32[2,8,1024]{2,1,0:T(8,128)S(1)}, f32[2,8,1024]{2,1,0:T(8,128)S(1)}, u32[]{:S(2)}, u32[]{:S(2)}) collective-permute-start(f32[2,8,1024]{2,1,0:T(8,128)S(1)} %bitcast.127), channel_id=1, source_target_pairs={{0,20},{2,22},{4,16},{6,18},{8,28},{10,30},{12,24},{14,26},{16,4},... | collective-permute-start | bytes 196616 | tf_op jit(solution)/shard_map/ppermute | solution.py:27
  24.6 3.6 %collective-permute-start.12 = (f32[2,8,1024]{2,1,0:T(8,128)S(1)}, f32[2,8,1024]{2,1,0:T(8,128)S(1)}, u32[]{:S(2)}, u32[]{:S(2)}) collective-permute-start(f32[2,8,1024]{2,1,0:T(8,128)S(1)} %bitcast.125), channel_id=1, source_target_pairs={{0,24},{2,26},{4,28},{6,30},{8,16},{10,18},{12,20},{14,22},{16,8},... | collective-permute-start | bytes 196616 | tf_op jit(solution)/shard_map/ppermute | solution.py:27
  28.2 3.7 %collective-permute-start.13 = (f32[2,8,1024]{2,1,0:T(8,128)S(1)}, f32[2,8,1024]{2,1,0:T(8,128)S(1)}, u32[]{:S(2)}, u32[]{:S(2)}) collective-permute-start(f32[2,8,1024]{2,1,0:T(8,128)S(1)} %bitcast.124), channel_id=1, source_target_pairs={{0,26},{2,24},{4,30},{6,28},{8,18},{10,16},{12,22},{14,20},{16,10}... | collective-permute-start | bytes 196616 | tf_op jit(solution)/shard_map/ppermute | solution.py:27
  31.9 0.6 collective-permute-done.9
  32.6 3.6 %collective-permute-start.14 = (f32[2,8,1024]{2,1,0:T(8,128)S(1)}, f32[2,8,1024]{2,1,0:T(8,128)S(1)}, u32[]{:S(2)}, u32[]{:S(2)}) collective-permute-start(f32[2,8,1024]{2,1,0:T(8,128)S(1)} %bitcast.123), channel_id=1, source_target_pairs={{0,28},{2,30},{4,24},{6,26},{8,20},{10,22},{12,16},{14,18},{16,12}... | collective-permute-start | bytes 196616 | tf_op jit(solution)/shard_map/ppermute | solution.py:27
  36.4 0.8 collective-permute-start.15
  37.2 0.6 collective-permute-done.11
  37.8 2.0 %collective-permute-done.14 = f32[2,8,1024]{2,1,0:T(8,128)S(1)} collective-permute-done((f32[2,8,1024]{2,1,0:T(8,128)S(1)}, f32[2,8,1024]{2,1,0:T(8,128)S(1)}, u32[]{:S(2)}, u32[]{:S(2)}) %collective-permute-start.14) | collective-permute-done | bytes 65568 | tf_op jit(solution)/shard_map/ppermute | solution.py:27
  39.9 3.5 %collective-permute-done.15 = f32[2,8,1024]{2,1,0:T(8,128)S(1)} collective-permute-done((f32[2,8,1024]{2,1,0:T(8,128)S(1)}, f32[2,8,1024]{2,1,0:T(8,128)S(1)}, u32[]{:S(2)}, u32[]{:S(2)}) %collective-permute-start.15) | collective-permute-done | bytes 65568 | tf_op jit(solution)/shard_map/ppermute | solution.py:27
  43.3 0.6 gather_fusion
  44.0 0.6 convolution_subtract_fusion
  44.6 0.7 convolution_bitcast_fusion
  45.4 0.8 copy.13
  46.2 30.6 %all_to_all.15 = f32[2,128,1024]{2,0,1:T(2,128)S(1)} all-to-all(f32[2,128,1024]{2,0,1:T(2,128)S(1)} %copy.13), channel_id=1, replica_groups=mesh['scan'=16,'row'=2] {'scan'}, dimensions={1} | all-to-all | bytes 2097152 | tf_op jit(solution)/shard_map/all_to_all | solution.py:93
  76.8 0.6 copy.48
  77.6 1.3 %collective-permute-start.16 = (f32[8,8,512]{2,1,0:T(8,128)S(1)}, f32[8,8,512]{2,1,0:T(8,128)S(1)}, u32[]{:S(2)}, u32[]{:S(2)}) collective-permute-start(f32[8,8,512]{2,1,0:T(8,128)S(1)} %slice_select_fusion), channel_id=1, source_target_pairs={{0,1},{1,0},{2,3},{3,2},{4,5},{5,4},{6,7},{7,6},{8,9},{9,8},{10,11... | collective-permute-start | bytes 393224 | tf_op jit(solution)/shard_map/ppermute | solution.py:39
  80.2 0.9 %reshape_squeeze.7 = f32[8,32,512]{2,1,0:T(8,128)} reshape(f32[1,8,16,1024]{3,2,1,0:T(8,128)S(1)} %get-tuple-element.4) | data formatting | bytes 1048576 | tf_op jit(solution)/shard_map/reshape;squeeze | solution.py:103
  81.1 2.8 %collective-permute-done.16 = f32[8,8,512]{2,1,0:T(8,128)S(1)} collective-permute-done((f32[8,8,512]{2,1,0:T(8,128)S(1)}, f32[8,8,512]{2,1,0:T(8,128)S(1)}, u32[]{:S(2)}, u32[]{:S(2)}) %collective-permute-start.16) | collective-permute-done | bytes 131104 | tf_op jit(solution)/shard_map/ppermute | solution.py:39
  83.9 1.6 %maximum_multiply_fusion = f32[8,32,512]{2,1,0:T(8,128)} fusion(f32[8,32,512]{2,1,0:T(8,128)S(1)} %copy-done, f32[8,8,512]{2,1,0:T(8,128)S(1)} %get-tuple-element.23, f32[8,32,512]{2,1,0:T(8,128)S(1)} %reshape_squeeze.6, f32[8,8,512]{2,1,0:T(8,128)S(1)} %get-tuple-element.22, f32[]{:T(128)S(6)} %mul.18, f32[]{:T(128)} %bitcast.115, ...), kind=kOutput, calls=%fused_computation.23 | convolution fusion | flops 76808192 | bytes 1841160 | tf_op jit(solution)/shard_map/rk,pkc->prc/dot_general | solution.py:59
  (69 shorter events, 2.2 us)
Async XLA Ops:
  0.6 8.0 %copy-start.3 = (f32[17]{0:T(128)S(1)}, f32[17]{0:T(128)}, u32[]{:S(2)}) copy-start(f32[17]{0:T(128)} %param.11) | copy-start | bytes 208
  0.6 7.7 %copy-start.1 = (f32[8,32,512]{2,1,0:T(8,128)S(1)}, f32[8,32,512]{2,1,0:T(8,128)}, u32[]{:S(2)}) copy-start(f32[8,32,512]{2,1,0:T(8,128)} %param.8) | copy-start | bytes 1572868
  0.7 8.1 %copy-start = (f32[8,32,512]{2,1,0:T(8,128)S(1)}, f32[8,32,512]{2,1,0:T(8,128)}, u32[]{:S(2)}) copy-start(f32[8,32,512]{2,1,0:T(8,128)} %param.7) | copy-start | bytes 1572868
  1.7 7.0 %collective-permute-start = (f32[8,8,512]{2,1,0:T(8,128)S(1)}, f32[8,8,512]{2,1,0:T(8,128)S(1)}, u32[]{:S(2)}, u32[]{:S(2)}) collective-permute-start(f32[8,8,512]{2,1,0:T(8,128)S(1)} %slice_select_fusion.1), channel_id=1, source_target_pairs={{0,1},{1,0},{2,3},{3,2},{4,5},{5,4},{6,7},{7,6},{8,9},{9,8},{10,11... | collective-permute-start | bytes 393224 | tf_op jit(solution)/shard_map/ppermute | solution.py:39
  11.0 4.1 %collective-permute-start.1 = (f32[2,8,1024]{2,1,0:T(8,128)S(1)}, f32[2,8,1024]{2,1,0:T(8,128)S(1)}, u32[]{:S(2)}, u32[]{:S(2)}) collective-permute-start(f32[2,8,1024]{2,1,0:T(8,128)S(1)} %bitcast.136), channel_id=1, source_target_pairs={{0,2},{2,0},{4,6},{6,4},{8,10},{10,8},{12,14},{14,12},{16,18},{18,... | collective-permute-start | bytes 196616 | tf_op jit(solution)/shard_map/ppermute | solution.py:27
  11.1 6.6 %collective-permute-start.2 = (f32[2,8,1024]{2,1,0:T(8,128)S(1)}, f32[2,8,1024]{2,1,0:T(8,128)S(1)}, u32[]{:S(2)}, u32[]{:S(2)}) collective-permute-start(f32[2,8,1024]{2,1,0:T(8,128)S(1)} %bitcast.135), channel_id=1, source_target_pairs={{0,4},{2,6},{4,0},{6,2},{8,12},{10,14},{12,8},{14,10},{16,20},{18,... | collective-permute-start | bytes 196616 | tf_op jit(solution)/shard_map/ppermute | solution.py:27
  12.7 5.3 %collective-permute-start.3 = (f32[2,8,1024]{2,1,0:T(8,128)S(1)}, f32[2,8,1024]{2,1,0:T(8,128)S(1)}, u32[]{:S(2)}, u32[]{:S(2)}) collective-permute-start(f32[2,8,1024]{2,1,0:T(8,128)S(1)} %bitcast.134), channel_id=1, source_target_pairs={{0,6},{2,4},{4,2},{6,0},{8,14},{10,12},{12,10},{14,8},{16,22},{18,... | collective-permute-start | bytes 196616 | tf_op jit(solution)/shard_map/ppermute | solution.py:27
  13.1 7.6 %collective-permute-start.4 = (f32[2,8,1024]{2,1,0:T(8,128)S(1)}, f32[2,8,1024]{2,1,0:T(8,128)S(1)}, u32[]{:S(2)}, u32[]{:S(2)}) collective-permute-start(f32[2,8,1024]{2,1,0:T(8,128)S(1)} %bitcast.133), channel_id=1, source_target_pairs={{0,8},{2,10},{4,12},{6,14},{8,0},{10,2},{12,4},{14,6},{16,24},{18,... | collective-permute-start | bytes 196616 | tf_op jit(solution)/shard_map/ppermute | solution.py:27
  14.8 6.4 %collective-permute-start.5 = (f32[2,8,1024]{2,1,0:T(8,128)S(1)}, f32[2,8,1024]{2,1,0:T(8,128)S(1)}, u32[]{:S(2)}, u32[]{:S(2)}) collective-permute-start(f32[2,8,1024]{2,1,0:T(8,128)S(1)} %bitcast.132), channel_id=1, source_target_pairs={{0,10},{2,8},{4,14},{6,12},{8,2},{10,0},{12,6},{14,4},{16,26},{18,... | collective-permute-start | bytes 196616 | tf_op jit(solution)/shard_map/ppermute | solution.py:27
  15.2 9.2 %collective-permute-start.6 = (f32[2,8,1024]{2,1,0:T(8,128)S(1)}, f32[2,8,1024]{2,1,0:T(8,128)S(1)}, u32[]{:S(2)}, u32[]{:S(2)}) collective-permute-start(f32[2,8,1024]{2,1,0:T(8,128)S(1)} %bitcast.131), channel_id=1, source_target_pairs={{0,12},{2,14},{4,8},{6,10},{8,4},{10,6},{12,0},{14,2},{16,28},{18,... | collective-permute-start | bytes 196616 | tf_op jit(solution)/shard_map/ppermute | solution.py:27
  17.8 6.8 %collective-permute-start.7 = (f32[2,8,1024]{2,1,0:T(8,128)S(1)}, f32[2,8,1024]{2,1,0:T(8,128)S(1)}, u32[]{:S(2)}, u32[]{:S(2)}) collective-permute-start(f32[2,8,1024]{2,1,0:T(8,128)S(1)} %bitcast.130), channel_id=1, source_target_pairs={{0,14},{2,12},{4,10},{6,8},{8,6},{10,4},{12,2},{14,0},{16,30},{18,... | collective-permute-start | bytes 196616 | tf_op jit(solution)/shard_map/ppermute | solution.py:27
  18.1 10.2 %collective-permute-start.8 = (f32[2,8,1024]{2,1,0:T(8,128)S(1)}, f32[2,8,1024]{2,1,0:T(8,128)S(1)}, u32[]{:S(2)}, u32[]{:S(2)}) collective-permute-start(f32[2,8,1024]{2,1,0:T(8,128)S(1)} %bitcast.129), channel_id=1, source_target_pairs={{0,16},{2,18},{4,20},{6,22},{8,24},{10,26},{12,28},{14,30},{16,0},... | collective-permute-start | bytes 196616 | tf_op jit(solution)/shard_map/ppermute | solution.py:27
  20.7 11.8 %collective-permute-start.9 = (f32[2,8,1024]{2,1,0:T(8,128)S(1)}, f32[2,8,1024]{2,1,0:T(8,128)S(1)}, u32[]{:S(2)}, u32[]{:S(2)}) collective-permute-start(f32[2,8,1024]{2,1,0:T(8,128)S(1)} %bitcast.128), channel_id=1, source_target_pairs={{0,18},{2,16},{4,22},{6,20},{8,26},{10,24},{12,30},{14,28},{16,2},... | collective-permute-start | bytes 196616 | tf_op jit(solution)/shard_map/ppermute | solution.py:27
  21.2 15.2 %collective-permute-start.10 = (f32[2,8,1024]{2,1,0:T(8,128)S(1)}, f32[2,8,1024]{2,1,0:T(8,128)S(1)}, u32[]{:S(2)}, u32[]{:S(2)}) collective-permute-start(f32[2,8,1024]{2,1,0:T(8,128)S(1)} %bitcast.127), channel_id=1, source_target_pairs={{0,20},{2,22},{4,16},{6,18},{8,28},{10,30},{12,24},{14,26},{16,4},... | collective-permute-start | bytes 196616 | tf_op jit(solution)/shard_map/ppermute | solution.py:27
  24.4 13.4 %collective-permute-start.11 = (f32[2,8,1024]{2,1,0:T(8,128)S(1)}, f32[2,8,1024]{2,1,0:T(8,128)S(1)}, u32[]{:S(2)}, u32[]{:S(2)}) collective-permute-start(f32[2,8,1024]{2,1,0:T(8,128)S(1)} %bitcast.126), channel_id=1, source_target_pairs={{0,22},{2,20},{4,18},{6,16},{8,30},{10,28},{12,26},{14,24},{16,6},... | collective-permute-start | bytes 196616 | tf_op jit(solution)/shard_map/ppermute | solution.py:27
  24.6 13.2 %collective-permute-start.12 = (f32[2,8,1024]{2,1,0:T(8,128)S(1)}, f32[2,8,1024]{2,1,0:T(8,128)S(1)}, u32[]{:S(2)}, u32[]{:S(2)}) collective-permute-start(f32[2,8,1024]{2,1,0:T(8,128)S(1)} %bitcast.125), channel_id=1, source_target_pairs={{0,24},{2,26},{4,28},{6,30},{8,16},{10,18},{12,20},{14,22},{16,8},... | collective-permute-start | bytes 196616 | tf_op jit(solution)/shard_map/ppermute | solution.py:27
  28.2 9.6 %collective-permute-start.13 = (f32[2,8,1024]{2,1,0:T(8,128)S(1)}, f32[2,8,1024]{2,1,0:T(8,128)S(1)}, u32[]{:S(2)}, u32[]{:S(2)}) collective-permute-start(f32[2,8,1024]{2,1,0:T(8,128)S(1)} %bitcast.124), channel_id=1, source_target_pairs={{0,26},{2,24},{4,30},{6,28},{8,18},{10,16},{12,22},{14,20},{16,10}... | collective-permute-start | bytes 196616 | tf_op jit(solution)/shard_map/ppermute | solution.py:27
  32.6 7.3 %collective-permute-start.14 = (f32[2,8,1024]{2,1,0:T(8,128)S(1)}, f32[2,8,1024]{2,1,0:T(8,128)S(1)}, u32[]{:S(2)}, u32[]{:S(2)}) collective-permute-start(f32[2,8,1024]{2,1,0:T(8,128)S(1)} %bitcast.123), channel_id=1, source_target_pairs={{0,28},{2,30},{4,24},{6,26},{8,20},{10,22},{12,16},{14,18},{16,12}... | collective-permute-start | bytes 196616 | tf_op jit(solution)/shard_map/ppermute | solution.py:27
  36.4 6.9 %collective-permute-start.15 = (f32[2,8,1024]{2,1,0:T(8,128)S(1)}, f32[2,8,1024]{2,1,0:T(8,128)S(1)}, u32[]{:S(2)}, u32[]{:S(2)}) collective-permute-start(f32[2,8,1024]{2,1,0:T(8,128)S(1)} %bitcast.122), channel_id=1, source_target_pairs={{0,30},{2,28},{4,26},{6,24},{8,22},{10,20},{12,18},{14,16},{16,14}... | collective-permute-start | bytes 196616 | tf_op jit(solution)/shard_map/ppermute | solution.py:27
  43.3 0.7 copy-start.2
  77.6 6.2 %collective-permute-start.16 = (f32[8,8,512]{2,1,0:T(8,128)S(1)}, f32[8,8,512]{2,1,0:T(8,128)S(1)}, u32[]{:S(2)}, u32[]{:S(2)}) collective-permute-start(f32[8,8,512]{2,1,0:T(8,128)S(1)} %slice_select_fusion), channel_id=1, source_target_pairs={{0,1},{1,0},{2,3},{3,2},{4,5},{5,4},{6,7},{7,6},{8,9},{9,8},{10,11... | collective-permute-start | bytes 393224 | tf_op jit(solution)/shard_map/ppermute | solution.py:39
